TPU v7x, 512 devices: a whole 4x4x16 slice. The times are simulated.
512 devices in a mesh: cfg: 2 (over core), grp: 4 (over y), seq: 64 (over x, z).
Axes of the slice: x: 4, y: 4, z: 16, core: 2. Of those that a mesh axis runs over, the one named last changes fastest.
Arguments:
- query: bfloat16 [2, 4, 2, 128, 2432], P('cfg', 'grp', None, 'seq'), may hold values from -150 to 150
- keys: bfloat16 [2, 4, 2, 128, 2432], P('cfg', 'grp', None, 'seq'), may hold values from -5.5 to 5.5
- values: bfloat16 [2, 4, 2, 128, 2432], P('cfg', 'grp', None, 'seq'), may hold values from -5 to 5
- hidden: bfloat16 [2, 4, 2, 128, 2432], P('cfg', 'grp', None, 'seq'), may hold values from -23 to 23
- latent: float32 [4, 2, 128, 64], P('grp', None, 'seq', 'cfg'), may hold values from -6 to 6
- deal: int32 [4, 2], replicated, may hold values from 0 to 5, as said below
- lengths: int32 [4, 2], replicated, may hold values from 64 to 128, as said below
- w_out: bfloat16 [2432, 2432], P(('cfg', 'seq')), may hold values from -0.125 to 0.125
- attn_gate: float32 [2, 6, 2432], P('cfg'), may hold values from 0.25 to 1.75
- modulation: float32 [2, 6, 2, 2432], P('cfg'), may hold values from -3 to 3
- w_final: bfloat16 [2432, 64], replicated, may hold values from -0.125 to 0.125
- guide: float32 [6], replicated, may hold values from 2 to 7
- step_size: float32 [6], replicated, may hold values from 0.15 to 0.5
Outputs:
- latent_next: float32 [4, 2, 128, 64], P('grp', None, 'seq', 'cfg')
Inputs may be any that keep to these rules, and one draw needn't show every extreme that they name: `deal`: column 0 of row g names the whole item of group g, column 1 the item split between groups g and g xor 1 (equal in both rows); every one of the 6 items is named by exactly one column-0 entry or one pair of column-1 entries. `lengths`: in each column some group has all 128 slots live.
All inputs are finite; a program needn't handle non-finite values.
Results may differ from a plain program's by a relative error of at most 0.0049.
Values may be sent and summed in bfloat16 or wider, within the bound.
No kernel may reach another device: no remote copies, remote signals or barrier semaphores. Data moves between devices by JAX's collectives and lax.ppermute only.
A program may use at most 128 MiB of HBM per device.

v0:
```python
import jax
import jax.numpy as jnp
from jax import lax
from jax.sharding import PartitionSpec as P

D = 2432
HEADS = 38
HD = 64
NORM_EPS = 1e-06


def from_partner(x, axis, apart):
    return lax.ppermute(x, axis, [(i, i ^ 1 << apart) for i in range(lax.axis_size(axis))])


def attend(queries, keys_all, values_all, live_keys):
    row_count = queries.shape[0]
    query_heads = queries.reshape(row_count, HEADS, HD)
    key_heads = keys_all.reshape(-1, HEADS, HD)
    value_heads = values_all.reshape(-1, HEADS, HD)
    scores = jnp.einsum(
        "shd,khd->hsk", query_heads, key_heads, preferred_element_type=jnp.float32
    ) * HD ** (-0.5)
    scores = jnp.where(live_keys[None, None, :], scores, -jnp.inf)
    peak_score = jnp.max(scores, axis=2, keepdims=True)
    raw_weights = jnp.exp(scores - peak_score)
    row_total = jnp.sum(raw_weights, axis=2, keepdims=True)
    weights = raw_weights.astype(jnp.bfloat16)
    mixed_out = (
        jnp.einsum("hsk,khd->hsd", weights, value_heads, preferred_element_type=jnp.float32)
        / row_total
    )
    return jnp.transpose(mixed_out, (1, 0, 2)).reshape(row_count, HEADS * HD)


def shards(
    query,
    keys,
    values,
    hidden,
    latent,
    deal,
    lengths,
    w_out,
    attn_gate,
    modulation,
    w_final,
    guide,
    step_size,
):
    group_id = lax.axis_index("grp")
    branch = lax.axis_index("cfg")
    partner = jnp.bitwise_xor(group_id, 1)
    own_lengths = lax.dynamic_index_in_dim(lengths, group_id, 0, keepdims=False)
    pair_lengths = lax.dynamic_index_in_dim(lengths, partner, 0, keepdims=False)
    item_ids = lax.dynamic_index_in_dim(deal, group_id, 0, keepdims=False)
    resident_key_rows = keys[0, 0]
    local_values = values[0, 0]
    shard_rows = resident_key_rows.shape[1]
    far_keys, far_values = from_partner((resident_key_rows[1], local_values[1]), "grp", 0)
    combined_key_rows, joint_values = (
        lax.all_gather(
            jnp.concatenate([resident_key_rows, far_keys[None]], 0), "seq", axis=1, tiled=True
        ),
        lax.all_gather(
            jnp.concatenate([local_values, far_values[None]], 0), "seq", axis=1, tiled=True
        ),
    )
    group_keys, group_values = (combined_key_rows[:2], joint_values[:2])
    pair_keys, pair_values = (combined_key_rows[2], joint_values[2])
    slot_total = group_keys.shape[1]
    slot_ids = jnp.arange(slot_total)
    live_home = slot_ids < own_lengths[0]
    live_own = slot_ids < own_lengths[1]
    live_pair = slot_ids < pair_lengths[1]
    local_query = query[0, 0]
    local_output_rows = attend(local_query[0], group_keys[0], group_values[0], live_home)
    shared = attend(
        local_query[1],
        jnp.concatenate([group_keys[1], pair_keys], 0),
        jnp.concatenate([group_values[1], pair_values], 0),
        jnp.concatenate([live_own, live_pair], 0),
    )
    attn_rows = (
        jnp.stack([local_output_rows, shared]).astype(jnp.bfloat16).reshape(2 * shard_rows, D)
    )
    projected = jnp.dot(
        attn_rows,
        lax.all_gather(w_out, ("cfg", "seq"), axis=0, tiled=True),
        preferred_element_type=jnp.float32,
    )
    projected = projected.reshape(2, shard_rows, D)
    item_count = guide.shape[0]
    indicator_mask = (jnp.arange(item_count)[None, :] == item_ids[:, None]).astype(jnp.float32)
    gate_now = jnp.einsum(
        "ri,id->rd", indicator_mask, attn_gate[0], precision=lax.Precision.HIGHEST
    )
    stream = hidden[0, 0].astype(jnp.float32) + gate_now[:, None, :] * projected
    row_mean = jnp.mean(stream, axis=2, keepdims=True)
    centred = stream - row_mean
    row_var = jnp.mean(centred * centred, axis=2, keepdims=True)
    normed = centred * lax.rsqrt(row_var + NORM_EPS)
    selected_entries = jnp.einsum(
        "ub,bkg->ukg", indicator_mask, modulation[0], precision=lax.Precision.HIGHEST
    )
    shaped = (
        normed * (1.0 + selected_entries[:, 1][:, None, :]) + selected_entries[:, 0][:, None, :]
    ).astype(jnp.bfloat16)
    velocity = jnp.einsum("rsd,dc->rsc", shaped, w_final, preferred_element_type=jnp.float32)
    row_slots = lax.axis_index("seq") * shard_rows + jnp.arange(shard_rows)
    live_rows = jnp.stack([row_slots < own_lengths[0], row_slots < own_lengths[1]])
    velocity = jnp.where(live_rows[:, :, None], velocity, jnp.float32(0.0))
    weight_now = jnp.sum(indicator_mask * guide[None, :], axis=1)[:, None, None]
    step_now = jnp.sum(indicator_mask * step_size[None, :], axis=1)[:, None, None]
    latent_part = latent[0]
    part_width = latent_part.shape[2]
    outgoing_velocity = lax.dynamic_slice_in_dim(velocity, (1 - branch) * part_width, part_width, 2)
    own_velocity = lax.dynamic_slice_in_dim(velocity, branch * part_width, part_width, 2)
    other_velocity = from_partner(outgoing_velocity, "cfg", 0)
    is_conditional = branch == 0
    cond_velocity = jnp.where(is_conditional, own_velocity, other_velocity)
    uncond_velocity = jnp.where(is_conditional, other_velocity, own_velocity)
    guided = uncond_velocity + weight_now * (cond_velocity - uncond_velocity)
    updated = latent_part - step_now * guided
    return updated[None]


def solution(mesh):
    placed = (
        P("cfg", "grp", None, "seq", None),
        P("cfg", "grp", None, "seq", None),
        P("cfg", "grp", None, "seq", None),
        P("cfg", "grp", None, "seq", None),
        P("grp", None, "seq", "cfg"),
        P(),
        P(),
        P(("cfg", "seq"), None),
        P("cfg", None, None),
        P("cfg", None, None, None),
        P(),
        P(),
        P(),
    )
    return jax.shard_map(
        shards, mesh=mesh, in_specs=placed, out_specs=P("grp", None, "seq", "cfg"), check_vma=False
    )
```

profile of v0, /device:TPU:1, one launch (start us, length us, event | category | flops | bytes accessed | tf_op | source)
XLA Modules:
  0.0 488.3 jit_solution(13304708734672202299)
XLA Ops:
  6.5 0.8 slice_bitcast_fusion.1
  7.3 4.0 collective-permute-start.1
  11.3 0.7 copy.77
  13.1 0.7 slice_bitcast_fusion.2
  13.8 3.4 collective-permute-start
  17.2 0.7 copy.78
  19.0 0.7 all-gather.9.cloned.1.call-update
  19.7 0.7 fusion.67
  20.5 0.8 constant_dynamic-slice_fusion.2
  21.9 0.9 fusion.57
  23.4 0.7 iota_compare_fusion.5
  24.1 1.3 iota_compare_fusion.3
  25.4 1.3 fusion.58
  26.8 1.0 fusion.34
  27.8 1.2 fusion.32
  29.0 122.6 %all-gather.7.cloned.1.call-done = bf16[3,128,2432]{2,0,1:T(4,128)(2,1)} async-done(((bf16[3,2,2432]{2,0,1:T(4,128)(2,1)}), bf16[3,128,2432]{2,0,1:T(4,128)(2,1)}) %all-gather.7.cloned.1.call-update) | async-done | bytes 1867792 | tf_op jit(solution)/shard_map/all_gather | solution.py:65
  151.6 7.6 %fusion.66 = (bf16[1,128,2432]{2,0,1:T(2,128)(2,1)S(1)}, bf16[1,128,2432]{2,0,1:T(2,128)(2,1)}, bf16[1,128,2432]{2,0,1:T(2,128)(2,1)S(1)}) fusion(bf16[3,128,2432]{2,0,1:T(4,128)(2,1)} %all-gather.7.cloned.1.call-done), kind=kLoop, calls=%fused_computation.84 | loop fusion | bytes 3735552 | tf_op jit(solution)/shard_map/slice | solution.py:77
  159.2 2.7 copy.57
  162.0 2.1 copy.56
  164.0 127.7 %all-gather.5.cloned.1.call-done = bf16[3,128,2432]{2,0,1:T(4,128)(2,1)} async-done(((bf16[3,2,2432]{2,0,1:T(4,128)(2,1)}), bf16[3,128,2432]{2,0,1:T(4,128)(2,1)}) %all-gather.5.cloned.1.call-update) | async-done | bytes 1867792 | tf_op jit(solution)/shard_map/all_gather | solution.py:62
  291.8 8.0 %fusion.65 = (bf16[1,128,2432]{2,0,1:T(2,128)(2,1)S(1)}, bf16[1,128,2432]{2,0,1:T(2,128)(2,1)}, bf16[1,128,2432]{2,0,1:T(2,128)(2,1)}) fusion(bf16[3,128,2432]{2,0,1:T(4,128)(2,1)} %all-gather.5.cloned.1.call-done), kind=kLoop, calls=%fused_computation.83 | loop fusion | bytes 3735552 | tf_op jit(solution)/shard_map/slice | solution.py:77
  299.8 3.6 copy.54
  303.4 3.6 copy.53
  306.9 1.7 fusion.69
  309.4 1.4 copy.51
  310.9 1.4 copy.47
  313.4 141.1 %all-gather.9.cloned.1.call-done = bf16[128,19,2432]{2,1,0:T(8,128)(2,1)} async-done(((bf16[1,19,2432]{2,1,0:T(8,128)(2,1)}), bf16[128,19,2432]{2,1,0:T(8,128)(2,1)}) %all-gather.9.cloned.1.call-update) | async-done | bytes 11829264 | tf_op jit(solution)/shard_map/all_gather | solution.py:89
  454.5 16.7 %reshape.76 = bf16[2432,2432,1]{1,0,2:T(8,128)(2,1)} reshape(bf16[128,19,2432]{2,1,0:T(8,128)(2,1)} %all-gather.9.cloned.1.call-done) | data formatting | bytes 23658496
  471.3 6.2 %fusion.71 = (f32[2,2]{1,0:T(2,128)S(1)}, f32[2,2,2432]{2,1,0:T(2,128)S(1)}) fusion(bf16[2432,2432,1]{1,0,2:T(8,128)(2,1)} %reshape.76, bf16[1,2,2432]{2,1,0:T(2,128)(2,1)S(1)} %stack_reshape.9, bf16[1,2,2432]{2,1,0:T(2,128)(2,1)S(1)} %stack_reshape.8, f32[2,2432]{1,0:T(2,128)S(1)} %fusion.34, bf16[1,1,2,2,2432]{4,3,2,1,0:T(2,128)(2,1)S(1)} %copy-done.2), kind=kOutput, calls=%fused_computation.89 | convolution fusion | flops 47394812 | bytes 11926544 | tf_op jit(solution)/shard_map/dot_general | solution.py:87
  478.1 2.2 collective-permute-start.2
  480.4 0.7 collective-permute-done.2
  481.1 0.7 fusion.55
  (45 shorter events, 6.1 us)
Async XLA Ops:
  6.5 471.2 %copy-start = (bf16[2432,64]{0,1:T(8,128)(2,1)S(1)}, bf16[2432,64]{0,1:T(8,128)(2,1)}, u32[]{:S(2)}) copy-start(bf16[2432,64]{0,1:T(8,128)(2,1)} %param.23) | copy-start | bytes 933892
  6.5 145.1 %all-gather.7.cloned.1.call-start = ((), (), s32[]{:S(2)}) async-start(), calls=%async_computation.1 | async-start | bytes 2529280 | tf_op jit(solution)/shard_map/all_gather | solution.py:65
  7.3 5.1 %collective-permute-start.1 = (bf16[2,2432]{1,0:T(2,128)(2,1)S(1)}, bf16[2,2432]{1,0:T(2,128)(2,1)S(1)}, u32[]{:S(2)}, u32[]{:S(2)}) collective-permute-start(bf16[2,2432]{1,0:T(2,128)(2,1)S(1)} %slice_bitcast_fusion.1), channel_id=1, source_target_pairs={{0,64},{64,0},{128,192},{192,128},{1,65},{65,1},{129,193},{193,129... | collective-permute-start | bytes 29192 | tf_op jit(solution)/shard_map/ppermute | solution.py:13
  13.1 278.7 %all-gather.5.cloned.1.call-start = ((), (), s32[]{:S(2)}) async-start(), calls=%async_computation | async-start | bytes 2529280 | tf_op jit(solution)/shard_map/all_gather | solution.py:62
  13.8 4.4 collective-permute-start
  18.9 435.6 %all-gather.9.cloned.1.call-start = ((), (), s32[]{:S(2)}) async-start(), calls=%async_computation.2 | async-start | bytes 15058944 | tf_op jit(solution)/shard_map/all_gather | solution.py:89
  306.9 1.9 copy-start.1
  313.4 157.8 %copy-start.2 = (bf16[1,1,2,2,2432]{4,3,2,1,0:T(2,128)(2,1)S(1)}, bf16[1,1,2,2,2432]{4,3,2,1,0:T(2,128)(2,1)}, u32[]{:S(2)}) copy-start(bf16[1,1,2,2,2432]{4,3,2,1,0:T(2,128)(2,1)} %param.16) | copy-start | bytes 58372
  471.2 9.0 %copy-start.4 = (f32[6]{0:T(128)S(1)}, f32[6]{0:T(128)}, u32[]{:S(2)}) copy-start(f32[6]{0:T(128)} %param.25) | copy-start | bytes 76
  471.2 9.0 %copy-start.5 = (f32[6]{0:T(128)S(1)}, f32[6]{0:T(128)}, u32[]{:S(2)}) copy-start(f32[6]{0:T(128)} %param.24) | copy-start | bytes 76
  471.2 9.9 %copy-start.3 = (f32[1,2,2,32]{3,2,1,0:T(2,128)S(1)}, f32[1,2,2,32]{3,2,1,0:T(2,128)}, u32[]{:S(2)}) copy-start(f32[1,2,2,32]{3,2,1,0:T(2,128)} %param.17) | copy-start | bytes 1540
  478.1 3.1 collective-permute-start.2
Sparse Core Ops, SparseCore 0:
  13.2 138.4 all-gather.6
  154.6 137.1 all-gather.4
  294.8 159.6 all-gather.8
where the time goes:
time: 490 us; the launch traced here: 488 us
  waiting for transfers between devices  393 us (80%)
  local copies, waits for them, and re-layouts  54.1 us (11%)
  between operations  13.3 us (3%)
  matrix products  11.7 us (2%)
  starting transfers between devices  9.63 us (2%)
  other arithmetic  6.06 us (1%)
    all_gather x1, waiting for transfers between devices, shards(): lax.all_gather(w_out, ('cfg', 'seq'), axis=0, tiled=True)  141 us
    all_gather x1, waiting for transfers between devices, shards(): lax.all_gather(jnp.concatenate([resident_key_rows, far_keys[None]], 0), '...  128 us
    all_gather x1, waiting for transfers between devices, shards(): lax.all_gather(jnp.concatenate([local_values, far_values[None]], 0), 'seq...  123 us
    unnamed x15, local copies, waits for them, and re-layouts  18.2 us
  transfers between devices with their start and end apart: 6, of which 6 were waited for; matrix products, arithmetic and copies ran while one was open for 9% of the time, Pallas kernels for 0%

commit v1 on v0

--- a/solution.py
+++ b/solution.py
@@ -59,8 +59,16 @@
     shard_rows = resident_key_rows.shape[1]
     far_keys, far_values = from_partner((resident_key_rows[1], local_values[1]), "grp", 0)
     combined_key_rows, joint_values = (
-        lax.all_gather(
-            jnp.concatenate([resident_key_rows, far_keys[None]], 0), "seq", axis=1, tiled=True
+        jnp.concatenate(
+            lax.all_to_all(
+                jnp.stack(
+                    [jnp.concatenate([resident_key_rows, far_keys[None]], 0)] * lax.axis_size("seq")
+                ),
+                "seq",
+                0,
+                0,
+            ),
+            axis=1,
         ),
         lax.all_gather(
             jnp.concatenate([local_values, far_values[None]], 0), "seq", axis=1, tiled=True

time: 490 us -> 362 us (0.74)
  waiting for transfers between devices: 393 us -> 252 us
  starting transfers between devices: 9.63 us -> 28 us
    all_gather x1 -> x0, waiting for transfers between devices: 128 us -> none  [shards(): lax.all_gather(jnp.concatenate([resident_key_rows, far_keys[None]], 0), '...]
    all_to_all x0 -> x1, starting transfers between devices: none -> 18.4 us  [shards(): lax.all_to_all(jnp.stack([jnp.concatenate([resident_key_rows, far_keys[No...]
    all_gather x1, waiting for transfers between devices: 141 us -> 131 us  [shards(): lax.all_gather(w_out, ('cfg', 'seq'), axis=0, tiled=True)]
    concatenate x0 -> x4, local copies, waits for them, and re-layouts: none -> 7.36 us  [shards(): jnp.concatenate([group_keys[1], pair_keys], 0)]
    slice x2 -> x1, local copies, waits for them, and re-layouts: 9.4 us -> 2.13 us  [shards(): group_keys[0]]
    unnamed x15 -> x30, local copies, waits for them, and re-layouts: 18.2 us -> 17.6 us
  transfers between devices with their start and end apart: 6 -> 6, of which waited for: 6 -> 5; matrix products, arithmetic and copies ran while one was open for 9% -> 12% of each run, Pallas kernels for 0% -> 0%
where the time goes in v1:
time: 362 us; the launch traced here: 361 us
  waiting for transfers between devices  252 us (70%)
  local copies, waits for them, and re-layouts  50.9 us (14%)
  starting transfers between devices  28 us (8%)
  between operations  13.7 us (4%)
  matrix products  10.3 us (3%)
  other arithmetic  5.99 us (2%)
    all_gather x1, waiting for transfers between devices, shards(): lax.all_gather(w_out, ('cfg', 'seq'), axis=0, tiled=True)  131 us
    all_gather x1, waiting for transfers between devices, shards(): lax.all_gather(jnp.concatenate([local_values, far_values[None]], 0), 'seq...  118 us
    all_to_all x1, starting transfers between devices, shards(): lax.all_to_all(jnp.stack([jnp.concatenate([resident_key_rows, far_keys[No...  18.4 us
    unnamed x30, local copies, waits for them, and re-layouts  17.6 us
    slice x2, local copies, waits for them, and re-layouts, shards(): group_values[0]  10 us
    ppermute x3, starting transfers between devices, from_partner(): lax.ppermute(x, axis, [(i, i ^ 1 << apart) for i in range(lax.axis_size(a...  9.55 us
    concatenate x4, local copies, waits for them, and re-layouts, shards(): jnp.concatenate([group_keys[1], pair_keys], 0)  7.36 us
  transfers between devices with their start and end apart: 6, of which 5 were waited for; matrix products, arithmetic and copies ran while one was open for 12% of the time, Pallas kernels for 0%

profile of v1, /device:TPU:1, one launch (start us, length us, event | category | flops | bytes accessed | tf_op | source)
XLA Modules:
  0.0 360.8 jit_solution(11261887712336749554)
XLA Ops:
  6.5 0.8 slice_bitcast_fusion.1
  7.3 4.0 %collective-permute-start.1 = (bf16[2,2432]{1,0:T(2,128)(2,1)S(1)}, bf16[2,2432]{1,0:T(2,128)(2,1)S(1)}, u32[]{:S(2)}, u32[]{:S(2)}) collective-permute-start(bf16[2,2432]{1,0:T(2,128)(2,1)S(1)} %slice_bitcast_fusion.1), channel_id=1, source_target_pairs={{0,64},{64,0},{128,192},{192,128},{1,65},{65,1},{129,193},{193,129... | collective-permute-start | bytes 29192 | tf_op jit(solution)/shard_map/ppermute | solution.py:13
  11.3 0.7 copy.81
  12.4 0.7 pad_maximum_fusion
  13.1 0.7 all-gather.6.cloned.1.call-update
  13.8 0.7 slice_bitcast_fusion.2
  14.5 3.4 collective-permute-start
  17.9 1.4 collective-permute-done
  19.3 0.8 pad_maximum_fusion.1
  20.1 2.2 stack.8
  22.3 18.4 %all-to-all-start = ((bf16[64,3,2,2432]{3,2,1,0:T(2,128)(2,1)}), bf16[64,3,2,2432]{3,2,1,0:T(2,128)(2,1)S(1)}, u32[]{:S(2)}, u32[]{:S(2)}) async-start(bf16[64,3,2,2432]{3,2,1,0:T(2,128)(2,1)} %stack.8), calls=%async_computation | async-start | bytes 3735552 | tf_op jit(solution)/shard_map/all_to_all | solution.py:63
  42.9 1.3 iota_compare_fusion.3
  44.3 1.2 fusion.67
  46.1 117.8 %all-gather.4.cloned.1.call-done = bf16[3,128,2432]{2,0,1:T(4,128)(2,1)} async-done(((bf16[3,2,2432]{2,0,1:T(4,128)(2,1)}), bf16[3,128,2432]{2,0,1:T(4,128)(2,1)}) %all-gather.4.cloned.1.call-update) | async-done | bytes 1867792 | tf_op jit(solution)/shard_map/all_gather | solution.py:73
  163.9 8.0 %fusion.74 = (bf16[1,128,2432]{2,0,1:T(2,128)(2,1)S(1)}, bf16[1,128,2432]{2,0,1:T(2,128)(2,1)}, bf16[1,128,2432]{2,0,1:T(2,128)(2,1)}) fusion(bf16[3,128,2432]{2,0,1:T(4,128)(2,1)} %all-gather.4.cloned.1.call-done), kind=kLoop, calls=%fused_computation.84 | loop fusion | bytes 3735552 | tf_op jit(solution)/shard_map/slice | solution.py:85
  171.9 3.6 copy.52
  175.4 3.6 copy.51
  179.0 2.0 copy.46
  181.1 2.1 fusion.75
  183.2 2.7 concatenate.29
  186.0 1.8 copy.49
  187.7 1.1 concatenate.28
  188.8 1.8 copy.48
  190.6 1.5 fusion.78
  193.0 1.1 reshape_squeeze.12
  194.0 0.8 fusion.79
  195.7 131.0 %all-gather.6.cloned.1.call-done = bf16[128,19,2432]{2,1,0:T(8,128)(2,1)} async-done(((bf16[1,19,2432]{2,1,0:T(8,128)(2,1)}), bf16[128,19,2432]{2,1,0:T(8,128)(2,1)}) %all-gather.6.cloned.1.call-update) | async-done | bytes 11829264 | tf_op jit(solution)/shard_map/all_gather | solution.py:97
  326.7 16.8 %reshape.90 = bf16[2432,2432,1]{1,0,2:T(8,128)(2,1)} reshape(bf16[128,19,2432]{2,1,0:T(8,128)(2,1)} %all-gather.6.cloned.1.call-done) | data formatting | bytes 23658496
  343.5 6.2 %fusion.80 = (f32[2,2]{1,0:T(2,128)S(1)}, f32[2,2,2432]{2,1,0:T(2,128)S(1)}) fusion(bf16[2432,2432,1]{1,0,2:T(8,128)(2,1)} %reshape.90, bf16[1,2,2432]{2,1,0:T(2,128)(2,1)S(1)} %stack_reshape.9, bf16[1,2,2432]{2,1,0:T(2,128)(2,1)S(1)} %stack_reshape.8, f32[2,2432]{1,0:T(2,128)S(1)} %fusion.43, bf16[1,1,2,2,2432]{4,3,2,1,0:T(2,128)(2,1)S(1)} %copy-done.7), kind=kOutput, calls=%fused_computation.90 | convolution fusion | flops 47394812 | bytes 11926544 | tf_op jit(solution)/shard_map/dot_general | solution.py:95
  350.3 2.2 collective-permute-start.2
  352.6 0.7 collective-permute-done.2
  353.3 0.7 fusion.64
  (61 shorter events, 5.4 us)
Async XLA Ops:
  6.5 343.4 %copy-start = (bf16[2432,64]{0,1:T(8,128)(2,1)S(1)}, bf16[2432,64]{0,1:T(8,128)(2,1)}, u32[]{:S(2)}) copy-start(bf16[2432,64]{0,1:T(8,128)(2,1)} %param.23) | copy-start | bytes 933892
  6.5 157.3 %all-gather.4.cloned.1.call-start = ((), (), s32[]{:S(2)}) async-start(), calls=%async_computation.1 | async-start | bytes 2529280 | tf_op jit(solution)/shard_map/all_gather | solution.py:73
  7.3 5.1 %collective-permute-start.1 = (bf16[2,2432]{1,0:T(2,128)(2,1)S(1)}, bf16[2,2432]{1,0:T(2,128)(2,1)S(1)}, u32[]{:S(2)}, u32[]{:S(2)}) collective-permute-start(bf16[2,2432]{1,0:T(2,128)(2,1)S(1)} %slice_bitcast_fusion.1), channel_id=1, source_target_pairs={{0,64},{64,0},{128,192},{192,128},{1,65},{65,1},{129,193},{193,129... | collective-permute-start | bytes 29192 | tf_op jit(solution)/shard_map/ppermute | solution.py:13
  13.1 313.6 %all-gather.6.cloned.1.call-start = ((), (), s32[]{:S(2)}) async-start(), calls=%async_computation.2 | async-start | bytes 15058944 | tf_op jit(solution)/shard_map/all_gather | solution.py:97
  14.5 4.7 %collective-permute-start = (bf16[2,2432]{1,0:T(2,128)(2,1)S(1)}, bf16[2,2432]{1,0:T(2,128)(2,1)S(1)}, u32[]{:S(2)}, u32[]{:S(2)}) collective-permute-start(bf16[2,2432]{1,0:T(2,128)(2,1)S(1)} %slice_bitcast_fusion.2), channel_id=1, source_target_pairs={{0,64},{64,0},{128,192},{192,128},{1,65},{65,1},{129,193},{193,129... | collective-permute-start | bytes 29192 | tf_op jit(solution)/shard_map/ppermute | solution.py:13
  22.3 18.5 %copy-start.8 = (bf16[1,1,2,2,2432]{4,3,2,1,0:T(2,128)(2,1)S(1)}, bf16[1,1,2,2,2432]{4,3,2,1,0:T(2,128)(2,1)}, u32[]{:S(2)}) copy-start(bf16[1,1,2,2,2432]{4,3,2,1,0:T(2,128)(2,1)} %param.13) | copy-start | bytes 58372
  22.3 18.6 %copy-start.9 = (s32[4,2]{0,1:T(2,128)S(1)}, s32[4,2]{0,1:T(2,128)}, u32[]{:S(2)}) copy-start(s32[4,2]{0,1:T(2,128)} %param.19) | copy-start | bytes 100
  22.3 19.3 %copy-start.11 = (s32[4,2]{0,1:T(2,128)S(1)}, s32[4,2]{0,1:T(2,128)}, u32[]{:S(2)}) copy-start(s32[4,2]{0,1:T(2,128)} %param.18) | copy-start | bytes 100
  22.3 23.2 %copy-start.6 = (f32[1,6,2432]{2,0,1:T(1,128)S(1)}, f32[1,6,2432]{2,0,1:T(1,128)}, u32[]{:S(2)}) copy-start(f32[1,6,2432]{2,0,1:T(1,128)} %param.21) | copy-start | bytes 175108
  22.3 23.5 %copy-start.5 = (f32[1,6,2,2432]{3,2,1,0:T(2,128)S(1)}, f32[1,6,2,2432]{3,2,1,0:T(2,128)}, u32[]{:S(2)}) copy-start(f32[1,6,2,2432]{3,2,1,0:T(2,128)} %param.22) | copy-start | bytes 350212
  22.3 158.8 %all-to-all-start = ((bf16[64,3,2,2432]{3,2,1,0:T(2,128)(2,1)}), bf16[64,3,2,2432]{3,2,1,0:T(2,128)(2,1)S(1)}, u32[]{:S(2)}, u32[]{:S(2)}) async-start(bf16[64,3,2,2432]{3,2,1,0:T(2,128)(2,1)} %stack.8), calls=%async_computation | async-start | bytes 3735552 | tf_op jit(solution)/shard_map/all_to_all | solution.py:63
  188.8 1.8 copy-start.4
  190.6 1.7 copy-start.2
  190.6 1.7 copy-start.3
  194.0 1.1 copy-start.1
  195.7 147.7 %copy-start.7 = (bf16[1,1,2,2,2432]{4,3,2,1,0:T(2,128)(2,1)S(1)}, bf16[1,1,2,2,2432]{4,3,2,1,0:T(2,128)(2,1)}, u32[]{:S(2)}) copy-start(bf16[1,1,2,2,2432]{4,3,2,1,0:T(2,128)(2,1)} %param.16) | copy-start | bytes 58372
  343.5 9.0 %copy-start.12 = (f32[6]{0:T(128)S(1)}, f32[6]{0:T(128)}, u32[]{:S(2)}) copy-start(f32[6]{0:T(128)} %param.25) | copy-start | bytes 76
  343.5 9.0 %copy-start.13 = (f32[6]{0:T(128)S(1)}, f32[6]{0:T(128)}, u32[]{:S(2)}) copy-start(f32[6]{0:T(128)} %param.24) | copy-start | bytes 76
  343.5 9.9 %copy-start.10 = (f32[1,2,2,32]{3,2,1,0:T(2,128)S(1)}, f32[1,2,2,32]{3,2,1,0:T(2,128)}, u32[]{:S(2)}) copy-start(f32[1,2,2,32]{3,2,1,0:T(2,128)} %param.17) | copy-start | bytes 1540
  350.3 3.1 collective-permute-start.2
Sparse Core Ops, SparseCore 0:
  13.2 150.6 all-gather.3
  166.9 159.7 all-gather.5
